TPU v7x, 512 devices: a whole 4x4x16 slice. The times are simulated.
512 devices in a mesh: section: 32 (over z_lo, y, core), seq: 16 (over x, z_hi).
Axes of the slice: x: 4, y: 4, z: 16 (z_hi: 4, z_lo: 4; z = z_hi * 4 + z_lo), core: 2. Of those that a mesh axis runs over, the one named last changes fastest.
Arguments:
- up_activation: bfloat16 [32, 2048, 4096], P('section', 'seq'), as said below
- saved_projections: bfloat16 [32, 2048, 768], P('section', 'seq'), as said below
- up_cotangent: bfloat16 [32, 2048, 4096], P('section', 'seq'), may hold values from -6 to 6
- up_input_weight: bfloat16 [32, 4096, 768], P('section', 'seq'), may hold values from -0.09375 to 0.09375
- up_output_weight: bfloat16 [32, 512, 4096], P('section', None, 'seq'), may hold values from -0.25 to 0.25
- upward_gain: float32 [32, 4096], P('section'), may hold values from 0.5 to 1.5
- accum_input: bfloat16 [32, 4096, 768], P('section', 'seq'), may hold values from -48 to 48
- doc_starts: int32 [32, 2048], P('section', 'seq'), may hold values from 0 to 2047, as said below
Outputs:
- upward_grad: bfloat16 [32, 2048, 4096], P('section', 'seq')
- project_grads: bfloat16 [32, 4096, 768], P('section', 'seq')
Inputs may be any that keep to these rules, and one draw needn't show every extreme that they name: doc_starts[s, t] is the position of the first token of the document holding token t: it is 0 at t = 0, equals t or doc_starts[s, t - 1] elsewhere, and the last token of every micro-batch starts a document. `up_activation`: saved inputs of the upward layers. `saved_projections`: saved queries, keys and values of the upward layers.
All inputs are finite; a program needn't handle non-finite values.
Results may differ from a plain program's by a relative error of at most 0.014.
Values may be sent and summed in bfloat16 or wider, within the bound.
No kernel may reach another device: no remote copies, remote signals or barrier semaphores. Data moves between devices by JAX's collectives and lax.ppermute only.
A program may use at most 64 MiB of HBM per device.

v0:
```python
import jax
import jax.numpy as jnp
from jax import lax
from jax.sharding import PartitionSpec as P

HEAD = 128
GROUP = 4
INNER = 4


def shifted(value, axis, steps):
    count = lax.axis_size(axis)
    initial, last = (max(0, -steps), min(count, count - steps))
    return lax.ppermute(value, axis, [(source, source + steps) for source in range(initial, last)])


def mirrored(value, axis):
    count = lax.axis_size(axis)
    return lax.ppermute(value, axis, [(source, count - 1 - source) for source in range(count)])


def seq_pairs(shift, level):
    size = lax.axis_size("seq")
    outer = size // INNER
    if level == 0:
        return [
            (o * INNER + i, o * INNER + (i + shift) % INNER)
            for o in range(outer)
            for i in range(INNER)
        ]
    return [
        (o * INNER + i, (o + shift) % outer * INNER + i) for o in range(outer) for i in range(INNER)
    ]


def gather_blocks(x):
    outer = lax.axis_size("seq") // INNER
    first = jnp.stack([x] + [lax.ppermute(x, "seq", seq_pairs(k, 0)) for k in range(1, INNER)])
    return jnp.stack(
        [first] + [lax.ppermute(first, "seq", seq_pairs(k, 1)) for k in range(1, outer)]
    )


def reduce_blocks(y, wire):
    outer = lax.axis_size("seq") // INNER
    acc = y[0]
    for k in range(1, outer):
        acc = acc + lax.ppermute(y[k].astype(wire), "seq", seq_pairs(outer - k, 1)).astype(y.dtype)
    total = acc[0]
    for k in range(1, INNER):
        total = total + lax.ppermute(acc[k].astype(wire), "seq", seq_pairs(INNER - k, 0)).astype(
            y.dtype
        )
    return total


def gather_and_scatter(x, cols, o, i):
    outer = lax.axis_size("seq") // INNER
    m, n, w = x.shape
    parts = cols.reshape(n, outer, INNER, w).transpose(2, 1, 0, 3)
    first = [jnp.concatenate([x, parts[i]])]
    for k in range(1, INNER):
        piece = lax.dynamic_index_in_dim(parts, (i + k) % INNER, 0, keepdims=False)
        first.append(lax.ppermute(jnp.concatenate([x, piece]), "seq", seq_pairs(k, 0)))
    first = jnp.stack(first, axis=1)
    own, rest = (first[:m], first[m:])
    second = []
    for k in range(1, outer):
        piece = lax.dynamic_index_in_dim(rest, (o + k) % outer, 0, keepdims=False)
        payload = jnp.concatenate([own.reshape(m * INNER, n, w), piece])
        second.append(lax.ppermute(payload, "seq", seq_pairs(k, 1)))
    gathered = jnp.stack([own] + [s[: m * INNER].reshape(m, INNER, n, w) for s in second])
    scattered = jnp.stack(
        [lax.dynamic_index_in_dim(rest, o, 0, keepdims=False)] + [s[m * INNER :] for s in second]
    )
    return (gathered, scattered)


def gather_columns(y, o, i):
    outer = lax.axis_size("seq") // INNER
    n, w = (y.shape[2], y.shape[3])
    first = [y[0]]
    for k in range(1, outer):
        first.append(lax.ppermute(y[k], "seq", seq_pairs(outer - k, 1)))
    first = jnp.stack(first, axis=1)
    second = [first[0]]
    for k in range(1, INNER):
        second.append(lax.ppermute(first[k], "seq", seq_pairs(INNER - k, 0)))
    second = jnp.stack(second, axis=1)
    second = jnp.roll(jnp.roll(second, o, axis=0), i, axis=1)
    return second.transpose(2, 0, 1, 3).reshape(n, outer * INNER * w)


def contract_last(left, right):
    return lax.dot_general(
        left, right, (((1,), (1,)), ((), ())), preferred_element_type=jnp.float32
    )


def contract_first(left, right):
    return lax.dot_general(
        left, right, (((0,), (0,)), ((), ())), preferred_element_type=jnp.float32
    )


def normalize(values, gain):
    floats = values.astype(jnp.float32)
    inverse = lax.rsqrt(jnp.mean(floats * floats, axis=-1, keepdims=True) + 1e-05)
    unit = floats * inverse
    return (unit, inverse, unit * gain)


def per_device(
    up_activation,
    saved_projections,
    up_cotangent,
    up_input_weight,
    up_output_weight,
    upward_gain,
    accum_input,
    doc_starts,
):
    factor = HEAD ** (-0.5)
    width = GROUP * HEAD
    count = up_activation.shape[1]
    size = lax.axis_size("seq")
    outer = size // INNER
    me = lax.axis_index("seq")
    o, i = (me // INNER, me % INNER)
    first = me * count
    saved = saved_projections[0]
    cotangent = up_cotangent[0]
    unit_up, inverse_up, normed_up = normalize(up_activation[0], upward_gain[0])
    hidden = normed_up.astype(jnp.bfloat16)
    output_weight = lax.all_gather(up_output_weight[0], "seq", axis=1, tiled=True)
    key_value = gather_blocks(saved[:, width:]).reshape(size * count, 2 * HEAD)
    kv_weight_all = lax.all_gather(up_input_weight[0][:, width:], "seq", axis=0, tiled=True)
    keys = key_value[:, :HEAD]
    values = key_value[:, HEAD:]
    sources = (
        ((o - jnp.arange(outer, dtype=jnp.int32)) % outer)[:, None] * INNER
        + ((i - jnp.arange(INNER, dtype=jnp.int32)) % INNER)[None, :]
    ).reshape(size)
    key_positions = (
        sources[:, None] * count + jnp.arange(count, dtype=jnp.int32)[None, :]
    ).reshape(-1)
    query = saved[:, :width].reshape(count, GROUP, HEAD)
    attn_grad = contract_last(cotangent, output_weight).astype(jnp.bfloat16)
    positions = first + jnp.arange(count, dtype=jnp.int32)
    starts = doc_starts[0]
    visible = (key_positions[None, :] <= positions[:, None]) & (
        key_positions[None, :] >= starts[:, None]
    )
    scores = jnp.einsum("tgh,jh->tgj", query, keys, preferred_element_type=jnp.float32) * factor
    scores = jnp.where(visible[:, None, :], scores, -1e30)
    top = jnp.max(scores, axis=-1, keepdims=True)
    exps = jnp.where(visible[:, None, :], jnp.exp(scores - top), 0.0)
    probs = exps / jnp.sum(exps, axis=-1, keepdims=True)
    weights = probs.astype(jnp.bfloat16)
    grad_heads = attn_grad.reshape(count, GROUP, HEAD)
    prob_grad = jnp.einsum("tgh,jh->tgj", grad_heads, values, preferred_element_type=jnp.float32)
    inner = jnp.sum(probs * prob_grad, axis=-1, keepdims=True)
    score_grad = (probs * (prob_grad - inner) * factor).astype(jnp.bfloat16)
    query_grad = (
        jnp.einsum("tgj,jh->tgh", score_grad, keys, preferred_element_type=jnp.float32)
        .astype(jnp.bfloat16)
        .reshape(count, width)
    )
    key_part = jnp.einsum("tgj,tgh->jh", score_grad, query, preferred_element_type=jnp.float32)
    value_part = jnp.einsum("tgj,tgh->jh", weights, grad_heads, preferred_element_type=jnp.float32)
    kv_part = jnp.concatenate([key_part, value_part], axis=1).reshape(outer, INNER, count, 2 * HEAD)
    query_all = gather_blocks(query_grad)
    kv_grad = reduce_blocks(kv_part, jnp.bfloat16).astype(jnp.bfloat16)
    kv_all, hidden_cols = gather_and_scatter(kv_grad[None], hidden, o, i)
    hidden_cols = hidden_cols.reshape(size * count, -1)
    grad_all = jnp.concatenate([query_all, kv_all[:, 0]], axis=-1).reshape(size * count, -1)
    input_term = contract_first(hidden_cols, grad_all).astype(jnp.bfloat16)
    block = contract_last(query_all.reshape(size * count, -1), up_input_weight[0][:, :width])
    hidden_grad = gather_columns(block.astype(jnp.bfloat16).reshape(outer, INNER, count, -1), o, i)
    hidden_grad = hidden_grad.astype(jnp.float32) + contract_last(kv_grad, kv_weight_all)
    scaled = hidden_grad * upward_gain[0]
    input_grad = cotangent.astype(jnp.float32) + inverse_up * (
        scaled - unit_up * jnp.mean(scaled * unit_up, axis=-1, keepdims=True)
    )
    moved_grad = shifted(input_grad.astype(jnp.bfloat16), "section", 1)
    mirror_input = mirrored(input_term, "section")
    project_grads = (accum_input[0].astype(jnp.float32) + mirror_input.astype(jnp.float32)).astype(
        jnp.bfloat16
    )
    return (moved_grad[None], project_grads[None])


def solution(mesh):
    return jax.shard_map(
        per_device,
        mesh=mesh,
        in_specs=(
            P("section", "seq", None),
            P("section", "seq", None),
            P("section", "seq", None),
            P("section", "seq", None),
            P("section", None, "seq"),
            P("section", None),
            P("section", "seq", None),
            P("section", "seq"),
        ),
        out_specs=(P("section", "seq", None), P("section", "seq", None)),
        check_vma=False,
    )
```

profile of v0, /device:TPU:43, one launch (start us, length us, event | category | flops | bytes accessed | tf_op | source)
XLA Modules:
  0.0 437.8 jit_solution(3843633651568549297)
XLA Ops:
  9.1 8.8 %collective-permute-start = (bf16[128,256]{0,1:T(8,128)(2,1)S(1)}, bf16[128,256]{0,1:T(8,128)(2,1)S(1)}, u32[]{:S(2)}, u32[]{:S(2)}) collective-permute-start(bf16[128,256]{0,1:T(8,128)(2,1)S(1)} %get-tuple-element.40), channel_id=1, source_target_pairs={{0,1},{1,2},{2,3},{3,0},{4,5},{5,6},{6,7},{7,4},{8,9},{9,10},{10,1... | collective-permute-start | bytes 196616 | tf_op jit(solution)/shard_map/ppermute | solution.py:38
  17.9 9.7 %collective-permute-start.1 = (bf16[128,256]{0,1:T(8,128)(2,1)S(1)}, bf16[128,256]{0,1:T(8,128)(2,1)S(1)}, u32[]{:S(2)}, u32[]{:S(2)}) collective-permute-start(bf16[128,256]{0,1:T(8,128)(2,1)S(1)} %get-tuple-element.40), channel_id=1, source_target_pairs={{0,2},{1,3},{2,0},{3,1},{4,6},{5,7},{6,4},{7,5},{8,10},{9,11},{10,... | collective-permute-start | bytes 196616 | tf_op jit(solution)/shard_map/ppermute | solution.py:38
  27.6 5.2 %collective-permute-start.2 = (bf16[128,256]{0,1:T(8,128)(2,1)S(1)}, bf16[128,256]{0,1:T(8,128)(2,1)S(1)}, u32[]{:S(2)}, u32[]{:S(2)}) collective-permute-start(bf16[128,256]{0,1:T(8,128)(2,1)S(1)} %get-tuple-element.40), channel_id=1, source_target_pairs={{0,3},{1,0},{2,1},{3,2},{4,7},{5,4},{6,5},{7,6},{8,11},{9,8},{10,9... | collective-permute-start | bytes 196616 | tf_op jit(solution)/shard_map/ppermute | solution.py:38
  34.7 5.3 %collective-permute-done.2 = bf16[128,256]{0,1:T(8,128)(2,1)S(1)} collective-permute-done((bf16[128,256]{0,1:T(8,128)(2,1)S(1)}, bf16[128,256]{0,1:T(8,128)(2,1)S(1)}, u32[]{:S(2)}, u32[]{:S(2)}) %collective-permute-start.2) | collective-permute-done | bytes 65568 | tf_op jit(solution)/shard_map/ppermute | solution.py:38
  40.0 3.1 collective-permute-start.3
  43.2 2.7 collective-permute-start.4
  45.9 3.8 collective-permute-start.5
  50.9 2.7 collective-permute-done.4
  53.6 6.2 %collective-permute-done.5 = bf16[4,128,256]{1,2,0:T(8,128)(2,1)S(1)} collective-permute-done((bf16[4,128,256]{1,2,0:T(8,128)(2,1)S(1)}, bf16[4,128,256]{1,2,0:T(8,128)(2,1)S(1)}, u32[]{:S(2)}, u32[]{:S(2)}) %collective-permute-start.5) | collective-permute-done | bytes 262176 | tf_op jit(solution)/shard_map/ppermute | solution.py:40
  60.5 3.7 fusion.88
  64.2 80.2 %all-gather.6.cloned.1.call-done = bf16[1,512,4096]{2,1,0:T(8,128)(2,1)} async-done(((bf16[1,512,256]{2,1,0:T(8,128)(2,1)}), bf16[1,512,4096]{2,1,0:T(8,128)(2,1)}) %all-gather.6.cloned.1.call-update) | async-done | bytes 4194320 | tf_op jit(solution)/shard_map/all_gather | solution.py:135
  144.5 3.7 fusion.38
  148.3 2.8 fusion.64
  152.7 7.6 %convolution_bitcast_fusion.1 = f32[2048,128]{0,1:T(8,128)S(1)} fusion(bf16[128,4,128]{0,2,1:T(8,128)(2,1)S(1)} %bitcast.230, f32[128,4,2048]{0,2,1:T(8,128)} %fusion.64, f32[128,4,2048]{0,2,1:T(8,128)} %get-tuple-element.46, f32[128,4]{0,1:T(4,128)S(1)} %get-tuple-element.45), kind=kOutput, calls=%fused_computation.27 | convolution fusion | flops 275778048 | bytes 9570304 | tf_op jit(solution)/shard_map/tgj,tgh->jh/dot_general | solution.py:169
  160.3 7.6 %fusion.41 = bf16[128,4,128]{0,2,1:T(8,128)(2,1)S(1)} fusion(f32[128,4,2048]{0,2,1:T(8,128)} %fusion.64, bf16[2048,256]{1,0:T(8,128)(2,1)} %bitcast.196, f32[128,4,2048]{0,2,1:T(8,128)} %get-tuple-element.46, f32[128,4]{0,1:T(4,128)S(1)} %get-tuple-element.45), kind=kOutput, calls=%fused_computation.59 | convolution fusion | flops 275843584 | bytes 17436672 | tf_op jit(solution)/shard_map/tgj,jh->tgh/dot_general | solution.py:165
  168.7 3.4 collective-permute-start.6
  172.2 6.4 %collective-permute-start.7 = (bf16[128,512]{1,0:T(8,128)(2,1)}, bf16[128,512]{1,0:T(8,128)(2,1)}, u32[]{:S(2)}, u32[]{:S(2)}) collective-permute-start(bf16[128,512]{1,0:T(8,128)(2,1)} %copy.48), channel_id=1, source_target_pairs={{0,2},{1,3},{2,0},{3,1},{4,6},{5,7},{6,4},{7,5},{8,10},{9,11},{10,... | collective-permute-start | bytes 393224 | tf_op jit(solution)/shard_map/ppermute | solution.py:38
  178.6 6.7 %collective-permute-start.8 = (bf16[128,512]{1,0:T(8,128)(2,1)}, bf16[128,512]{1,0:T(8,128)(2,1)}, u32[]{:S(2)}, u32[]{:S(2)}) collective-permute-start(bf16[128,512]{1,0:T(8,128)(2,1)} %copy.48), channel_id=1, source_target_pairs={{0,3},{1,0},{2,1},{3,2},{4,7},{5,4},{6,5},{7,6},{8,11},{9,8},{10,9... | collective-permute-start | bytes 393224 | tf_op jit(solution)/shard_map/ppermute | solution.py:38
  186.3 2.2 collective-permute-start.18
  189.3 4.2 collective-permute-start.19
  194.3 3.4 collective-permute-start.20
  209.8 3.6 collective-permute-start.10
  213.5 3.2 collective-permute-start.11
  216.8 2.2 fusion.85
  219.0 3.3 collective-permute-start.21
  222.3 2.2 fusion.22
  224.5 6.4 %collective-permute-start.22 = (bf16[128,256]{1,0:T(8,128)(2,1)S(1)}, bf16[128,256]{1,0:T(8,128)(2,1)S(1)}, u32[]{:S(2)}, u32[]{:S(2)}) collective-permute-start(bf16[128,256]{1,0:T(8,128)(2,1)S(1)} %get-tuple-element.36), channel_id=1, source_target_pairs={{0,2},{1,3},{2,0},{3,1},{4,6},{5,7},{6,4},{7,5},{8,10},{9,11},{10,... | collective-permute-start | bytes 196616 | tf_op jit(solution)/shard_map/ppermute | solution.py:51
  230.9 6.5 %collective-permute-start.23 = (bf16[128,256]{1,0:T(8,128)(2,1)S(1)}, bf16[128,256]{1,0:T(8,128)(2,1)S(1)}, u32[]{:S(2)}, u32[]{:S(2)}) collective-permute-start(bf16[128,256]{1,0:T(8,128)(2,1)S(1)} %get-tuple-element.35), channel_id=1, source_target_pairs={{0,1},{1,2},{2,3},{3,0},{4,5},{5,6},{6,7},{7,4},{8,9},{9,10},{10,1... | collective-permute-start | bytes 196616 | tf_op jit(solution)/shard_map/ppermute | solution.py:51
  238.9 5.3 %collective-permute-done.22 = bf16[128,256]{1,0:T(8,128)(2,1)S(1)} collective-permute-done((bf16[128,256]{1,0:T(8,128)(2,1)S(1)}, bf16[128,256]{1,0:T(8,128)(2,1)S(1)}, u32[]{:S(2)}, u32[]{:S(2)}) %collective-permute-start.22) | collective-permute-done | bytes 65568 | tf_op jit(solution)/shard_map/ppermute | solution.py:51
  245.2 12.0 %collective-permute-start.25 = (bf16[5,128,256]{2,1,0:T(8,128)(2,1)S(1)}, bf16[5,128,256]{2,1,0:T(8,128)(2,1)S(1)}, u32[]{:S(2)}, u32[]{:S(2)}) collective-permute-start(bf16[5,128,256]{2,1,0:T(8,128)(2,1)S(1)} %get-tuple-element.42), channel_id=1, source_target_pairs={{0,1},{1,2},{2,3},{3,0},{4,5},{5,6},{6,7},{7,4},{8,9},{9,10},{10,1... | collective-permute-start | bytes 983048 | tf_op jit(solution)/shard_map/ppermute | solution.py:64
  257.2 8.0 %collective-permute-start.26 = (bf16[5,128,256]{2,1,0:T(8,128)(2,1)S(1)}, bf16[5,128,256]{2,1,0:T(8,128)(2,1)S(1)}, u32[]{:S(2)}, u32[]{:S(2)}) collective-permute-start(bf16[5,128,256]{2,1,0:T(8,128)(2,1)S(1)} %get-tuple-element.43), channel_id=1, source_target_pairs={{0,2},{1,3},{2,0},{3,1},{4,6},{5,7},{6,4},{7,5},{8,10},{9,11},{10,... | collective-permute-start | bytes 983048 | tf_op jit(solution)/shard_map/ppermute | solution.py:64
  271.6 5.7 %collective-permute-start.13 = (bf16[4,128,256]{2,1,0:T(8,128)(2,1)S(1)}, bf16[4,128,256]{2,1,0:T(8,128)(2,1)S(1)}, u32[]{:S(2)}, u32[]{:S(2)}) collective-permute-start(bf16[4,128,256]{2,1,0:T(8,128)(2,1)S(1)} %bitcast.221), channel_id=1, source_target_pairs={{0,8},{1,9},{2,10},{3,11},{4,12},{5,13},{6,14},{7,15},{8,0},{9,1},... | collective-permute-start | bytes 786440 | tf_op jit(solution)/shard_map/ppermute | solution.py:84
  277.3 17.4 %collective-permute-done.25 = bf16[5,128,256]{2,1,0:T(8,128)(2,1)S(1)} collective-permute-done((bf16[5,128,256]{2,1,0:T(8,128)(2,1)S(1)}, bf16[5,128,256]{2,1,0:T(8,128)(2,1)S(1)}, u32[]{:S(2)}, u32[]{:S(2)}) %collective-permute-start.25) | collective-permute-done | bytes 327712 | tf_op jit(solution)/shard_map/ppermute | solution.py:64
  294.7 5.9 %collective-permute-start.14 = (bf16[4,128,256]{2,1,0:T(8,128)(2,1)S(1)}, bf16[4,128,256]{2,1,0:T(8,128)(2,1)S(1)}, u32[]{:S(2)}, u32[]{:S(2)}) collective-permute-start(bf16[4,128,256]{2,1,0:T(8,128)(2,1)S(1)} %bitcast.219), channel_id=1, source_target_pairs={{0,4},{1,5},{2,6},{3,7},{4,8},{5,9},{6,10},{7,11},{8,12},{9,13},{1... | collective-permute-start | bytes 786440 | tf_op jit(solution)/shard_map/ppermute | solution.py:84
  301.0 4.8 %collective-permute-done.14 = bf16[4,128,256]{2,1,0:T(8,128)(2,1)S(1)} collective-permute-done((bf16[4,128,256]{2,1,0:T(8,128)(2,1)S(1)}, bf16[4,128,256]{2,1,0:T(8,128)(2,1)S(1)}, u32[]{:S(2)}, u32[]{:S(2)}) %collective-permute-start.14) | collective-permute-done | bytes 262176 | tf_op jit(solution)/shard_map/ppermute | solution.py:84
  306.0 4.9 %collective-permute-start.15 = (bf16[4,128,256]{2,1,0:T(8,128)(2,1)S(1)}, bf16[4,128,256]{2,1,0:T(8,128)(2,1)S(1)}, u32[]{:S(2)}, u32[]{:S(2)}) collective-permute-start(bf16[4,128,256]{2,1,0:T(8,128)(2,1)S(1)} %get-tuple-element.16), channel_id=1, source_target_pairs={{0,3},{1,0},{2,1},{3,2},{4,7},{5,4},{6,5},{7,6},{8,11},{9,8},{10,9... | collective-permute-start | bytes 786440 | tf_op jit(solution)/shard_map/ppermute | solution.py:88
  311.0 5.1 %collective-permute-start.16 = (bf16[4,128,256]{2,1,0:T(8,128)(2,1)S(1)}, bf16[4,128,256]{2,1,0:T(8,128)(2,1)S(1)}, u32[]{:S(2)}, u32[]{:S(2)}) collective-permute-start(bf16[4,128,256]{2,1,0:T(8,128)(2,1)S(1)} %get-tuple-element.18), channel_id=1, source_target_pairs={{0,2},{1,3},{2,0},{3,1},{4,6},{5,7},{6,4},{7,5},{8,10},{9,11},{10,... | collective-permute-start | bytes 786440 | tf_op jit(solution)/shard_map/ppermute | solution.py:88
  316.1 5.4 %collective-permute-start.17 = (bf16[4,128,256]{2,1,0:T(8,128)(2,1)S(1)}, bf16[4,128,256]{2,1,0:T(8,128)(2,1)S(1)}, u32[]{:S(2)}, u32[]{:S(2)}) collective-permute-start(bf16[4,128,256]{2,1,0:T(8,128)(2,1)S(1)} %get-tuple-element.15), channel_id=1, source_target_pairs={{0,1},{1,2},{2,3},{3,0},{4,5},{5,6},{6,7},{7,4},{8,9},{9,10},{10,1... | collective-permute-start | bytes 786440 | tf_op jit(solution)/shard_map/ppermute | solution.py:88
  323.5 6.1 %collective-permute-start.28 = (bf16[8,128,256]{2,1,0:T(8,128)(2,1)}, bf16[8,128,256]{2,1,0:T(8,128)(2,1)}, u32[]{:S(2)}, u32[]{:S(2)}) collective-permute-start(bf16[8,128,256]{2,1,0:T(8,128)(2,1)} %get-tuple-element.31), channel_id=1, source_target_pairs={{0,4},{1,5},{2,6},{3,7},{4,8},{5,9},{6,10},{7,11},{8,12},{9,13},{1... | collective-permute-start | bytes 1572872 | tf_op jit(solution)/shard_map/ppermute | solution.py:71
  329.7 5.4 %collective-permute-start.29 = (bf16[8,128,256]{2,1,0:T(8,128)(2,1)}, bf16[8,128,256]{2,1,0:T(8,128)(2,1)}, u32[]{:S(2)}, u32[]{:S(2)}) collective-permute-start(bf16[8,128,256]{2,1,0:T(8,128)(2,1)} %get-tuple-element.32), channel_id=1, source_target_pairs={{0,8},{1,9},{2,10},{3,11},{4,12},{5,13},{6,14},{7,15},{8,0},{9,1},... | collective-permute-start | bytes 1572872 | tf_op jit(solution)/shard_map/ppermute | solution.py:71
  335.0 7.3 %collective-permute-done.15 = bf16[4,128,256]{2,1,0:T(8,128)(2,1)S(1)} collective-permute-done((bf16[4,128,256]{2,1,0:T(8,128)(2,1)S(1)}, bf16[4,128,256]{2,1,0:T(8,128)(2,1)S(1)}, u32[]{:S(2)}, u32[]{:S(2)}) %collective-permute-start.15) | collective-permute-done | bytes 262176 | tf_op jit(solution)/shard_map/ppermute | solution.py:88
  342.3 2.2 collective-permute-start.30
  344.5 13.3 %collective-permute-done.16 = bf16[4,128,256]{2,1,0:T(8,128)(2,1)S(1)} collective-permute-done((bf16[4,128,256]{2,1,0:T(8,128)(2,1)S(1)}, bf16[4,128,256]{2,1,0:T(8,128)(2,1)S(1)}, u32[]{:S(2)}, u32[]{:S(2)}) %collective-permute-start.16) | collective-permute-done | bytes 262176 | tf_op jit(solution)/shard_map/ppermute | solution.py:88
  362.8 3.2 multiply_reduce_fusion.1
  366.8 4.1 collective-permute-start.24
  374.4 2.4 fusion.35
  376.8 34.8 %collective-permute-start.31 = (bf16[256,768]{1,0:T(8,128)(2,1)S(1)}, bf16[256,768]{1,0:T(8,128)(2,1)S(1)}, u32[]{:S(2)}, u32[]{:S(2)}) collective-permute-start(bf16[256,768]{1,0:T(8,128)(2,1)S(1)} %fusion.35), channel_id=1, source_target_pairs={{0,496},{16,480},{32,464},{48,448},{64,432},{80,416},{96,400},{112... | collective-permute-start | bytes 1179656 | tf_op jit(solution)/shard_map/ppermute | solution.py:19
  411.7 17.4 %collective-permute-done.31 = bf16[256,768]{1,0:T(8,128)(2,1)S(1)} collective-permute-done((bf16[256,768]{1,0:T(8,128)(2,1)S(1)}, bf16[256,768]{1,0:T(8,128)(2,1)S(1)}, u32[]{:S(2)}, u32[]{:S(2)}) %collective-permute-start.31) | collective-permute-done | bytes 393248 | tf_op jit(solution)/shard_map/ppermute | solution.py:19
  (125 shorter events, 44.8 us)
Async XLA Ops:
  7.2 42.5 %copy-start.15 = (s32[1,128]{1,0:T(1,128)S(1)}, s32[1,128]{1,0:T(1,128)}, u32[]{:S(2)}) copy-start(s32[1,128]{1,0:T(1,128)} %param.15) | copy-start | bytes 1540
  7.2 42.9 %copy-start = (bf16[1,128,4096]{2,1,0:T(8,128)(2,1)S(1)}, bf16[1,128,4096]{2,1,0:T(8,128)(2,1)}, u32[]{:S(2)}) copy-start(bf16[1,128,4096]{2,1,0:T(8,128)(2,1)} %param.8) | copy-start | bytes 3145732
  7.2 137.3 %all-gather.6.cloned.1.call-start = ((), (), s32[]{:S(2)}) async-start(), calls=%async_computation.1 | async-start | bytes 4456448 | tf_op jit(solution)/shard_map/all_gather | solution.py:135
  7.9 354.9 %all-gather.4.cloned.1.call-start = ((), (), s32[]{:S(2)}) async-start(), calls=%async_computation | async-start | bytes 2228224 | tf_op jit(solution)/shard_map/all_gather | solution.py:137
  9.1 25.6 %collective-permute-start = (bf16[128,256]{0,1:T(8,128)(2,1)S(1)}, bf16[128,256]{0,1:T(8,128)(2,1)S(1)}, u32[]{:S(2)}, u32[]{:S(2)}) collective-permute-start(bf16[128,256]{0,1:T(8,128)(2,1)S(1)} %get-tuple-element.40), channel_id=1, source_target_pairs={{0,1},{1,2},{2,3},{3,0},{4,5},{5,6},{6,7},{7,4},{8,9},{9,10},{10,1... | collective-permute-start | bytes 196616 | tf_op jit(solution)/shard_map/ppermute | solution.py:38
  17.9 16.8 %collective-permute-start.1 = (bf16[128,256]{0,1:T(8,128)(2,1)S(1)}, bf16[128,256]{0,1:T(8,128)(2,1)S(1)}, u32[]{:S(2)}, u32[]{:S(2)}) collective-permute-start(bf16[128,256]{0,1:T(8,128)(2,1)S(1)} %get-tuple-element.40), channel_id=1, source_target_pairs={{0,2},{1,3},{2,0},{3,1},{4,6},{5,7},{6,4},{7,5},{8,10},{9,11},{10,... | collective-permute-start | bytes 196616 | tf_op jit(solution)/shard_map/ppermute | solution.py:38
  27.6 12.3 %collective-permute-start.2 = (bf16[128,256]{0,1:T(8,128)(2,1)S(1)}, bf16[128,256]{0,1:T(8,128)(2,1)S(1)}, u32[]{:S(2)}, u32[]{:S(2)}) collective-permute-start(bf16[128,256]{0,1:T(8,128)(2,1)S(1)} %get-tuple-element.40), channel_id=1, source_target_pairs={{0,3},{1,0},{2,1},{3,2},{4,7},{5,4},{6,5},{7,6},{8,11},{9,8},{10,9... | collective-permute-start | bytes 196616 | tf_op jit(solution)/shard_map/ppermute | solution.py:38
  40.0 10.9 %collective-permute-start.3 = (bf16[4,128,256]{1,2,0:T(8,128)(2,1)S(1)}, bf16[4,128,256]{1,2,0:T(8,128)(2,1)S(1)}, u32[]{:S(2)}, u32[]{:S(2)}) collective-permute-start(bf16[4,128,256]{1,2,0:T(8,128)(2,1)S(1)} %get-tuple-element.38), channel_id=1, source_target_pairs={{0,4},{1,5},{2,6},{3,7},{4,8},{5,9},{6,10},{7,11},{8,12},{9,13},{1... | collective-permute-start | bytes 786440 | tf_op jit(solution)/shard_map/ppermute | solution.py:40
  43.2 10.4 %collective-permute-start.4 = (bf16[4,128,256]{1,2,0:T(8,128)(2,1)S(1)}, bf16[4,128,256]{1,2,0:T(8,128)(2,1)S(1)}, u32[]{:S(2)}, u32[]{:S(2)}) collective-permute-start(bf16[4,128,256]{1,2,0:T(8,128)(2,1)S(1)} %get-tuple-element.38), channel_id=1, source_target_pairs={{0,8},{1,9},{2,10},{3,11},{4,12},{5,13},{6,14},{7,15},{8,0},{9,1},... | collective-permute-start | bytes 786440 | tf_op jit(solution)/shard_map/ppermute | solution.py:40
  45.9 13.9 %collective-permute-start.5 = (bf16[4,128,256]{1,2,0:T(8,128)(2,1)S(1)}, bf16[4,128,256]{1,2,0:T(8,128)(2,1)S(1)}, u32[]{:S(2)}, u32[]{:S(2)}) collective-permute-start(bf16[4,128,256]{1,2,0:T(8,128)(2,1)S(1)} %get-tuple-element.38), channel_id=1, source_target_pairs={{0,12},{1,13},{2,14},{3,15},{4,0},{5,1},{6,2},{7,3},{8,4},{9,5},{1... | collective-permute-start | bytes 786440 | tf_op jit(solution)/shard_map/ppermute | solution.py:40
  60.5 87.9 %copy-start.5 = (bf16[4,4,128,256]{3,2,1,0:T(8,128)(2,1)}, bf16[4,4,128,256]{3,2,1,0:T(8,128)(2,1)S(1)}, u32[]{:S(2)}) copy-start(bf16[4,4,128,256]{3,2,1,0:T(8,128)(2,1)S(1)} %copy.41) | copy-start | bytes 3145732
  60.5 84.0 %copy-start.3 = (bf16[1,128,4096]{2,1,0:T(8,128)(2,1)S(1)}, bf16[1,128,4096]{2,1,0:T(8,128)(2,1)}, u32[]{:S(2)}) copy-start(bf16[1,128,4096]{2,1,0:T(8,128)(2,1)} %param.10) | copy-start | bytes 3145732
  148.3 3.5 copy-start.17
  152.7 32.5 %copy-start.1 = (f32[2048,128]{0,1:T(8,128)}, f32[2048,128]{0,1:T(8,128)S(1)}, u32[]{:S(2)}) copy-start(f32[2048,128]{0,1:T(8,128)S(1)} %convolution_bitcast_fusion) | copy-start | bytes 3145732
  160.3 24.9 %copy-start.2 = (f32[2048,128]{0,1:T(8,128)}, f32[2048,128]{0,1:T(8,128)S(1)}, u32[]{:S(2)}) copy-start(f32[2048,128]{0,1:T(8,128)S(1)} %convolution_bitcast_fusion.1) | copy-start | bytes 3145732
  168.7 25.6 %collective-permute-start.6 = (bf16[128,512]{1,0:T(8,128)(2,1)}, bf16[128,512]{1,0:T(8,128)(2,1)S(1)}, u32[]{:S(2)}, u32[]{:S(2)}) collective-permute-start(bf16[128,512]{1,0:T(8,128)(2,1)} %copy.48), channel_id=1, source_target_pairs={{0,1},{1,2},{2,3},{3,0},{4,5},{5,6},{6,7},{7,4},{8,9},{9,10},{10,1... | collective-permute-start | bytes 393224 | tf_op jit(solution)/shard_map/ppermute | solution.py:38
  172.2 33.7 %collective-permute-start.7 = (bf16[128,512]{1,0:T(8,128)(2,1)}, bf16[128,512]{1,0:T(8,128)(2,1)}, u32[]{:S(2)}, u32[]{:S(2)}) collective-permute-start(bf16[128,512]{1,0:T(8,128)(2,1)} %copy.48), channel_id=1, source_target_pairs={{0,2},{1,3},{2,0},{3,1},{4,6},{5,7},{6,4},{7,5},{8,10},{9,11},{10,... | collective-permute-start | bytes 393224 | tf_op jit(solution)/shard_map/ppermute | solution.py:38
  178.6 27.3 %collective-permute-start.8 = (bf16[128,512]{1,0:T(8,128)(2,1)}, bf16[128,512]{1,0:T(8,128)(2,1)}, u32[]{:S(2)}, u32[]{:S(2)}) collective-permute-start(bf16[128,512]{1,0:T(8,128)(2,1)} %copy.48), channel_id=1, source_target_pairs={{0,3},{1,0},{2,1},{3,2},{4,7},{5,4},{6,5},{7,6},{8,11},{9,8},{10,9... | collective-permute-start | bytes 393224 | tf_op jit(solution)/shard_map/ppermute | solution.py:38
  185.4 12.4 %copy-start.16 = (f32[128]{0:T(128)S(1)}, f32[128]{0:T(128)}, u32[]{:S(2)}) copy-start(f32[128]{0:T(128)} %fusion.20) | copy-start | bytes 1540
  186.3 27.2 %collective-permute-start.18 = (bf16[4,128,256]{2,1,0:T(8,128)(2,1)}, bf16[4,128,256]{2,1,0:T(8,128)(2,1)}, u32[]{:S(2)}, u32[]{:S(2)}) collective-permute-start(bf16[4,128,256]{2,1,0:T(8,128)(2,1)} %bitcast.49), channel_id=1, source_target_pairs={{0,12},{1,13},{2,14},{3,15},{4,0},{5,1},{6,2},{7,3},{8,4},{9,5},{1... | collective-permute-start | bytes 786440 | tf_op jit(solution)/shard_map/ppermute | solution.py:48
  188.5 12.0 %copy-start.10 = (f32[1,4096]{1,0:T(1,128)S(1)}, f32[1,4096]{1,0:T(1,128)}, u32[]{:S(2)}) copy-start(f32[1,4096]{1,0:T(1,128)} %param.13) | copy-start | bytes 49156
  189.3 27.4 %collective-permute-start.19 = (bf16[4,128,256]{2,1,0:T(8,128)(2,1)}, bf16[4,128,256]{2,1,0:T(8,128)(2,1)}, u32[]{:S(2)}, u32[]{:S(2)}) collective-permute-start(bf16[4,128,256]{2,1,0:T(8,128)(2,1)} %bitcast.50), channel_id=1, source_target_pairs={{0,8},{1,9},{2,10},{3,11},{4,12},{5,13},{6,14},{7,15},{8,0},{9,1},... | collective-permute-start | bytes 786440 | tf_op jit(solution)/shard_map/ppermute | solution.py:48
  194.3 22.4 %collective-permute-start.20 = (bf16[4,128,256]{2,1,0:T(8,128)(2,1)}, bf16[4,128,256]{2,1,0:T(8,128)(2,1)}, u32[]{:S(2)}, u32[]{:S(2)}) collective-permute-start(bf16[4,128,256]{2,1,0:T(8,128)(2,1)} %bitcast.51), channel_id=1, source_target_pairs={{0,4},{1,5},{2,6},{3,7},{4,8},{5,9},{6,10},{7,11},{8,12},{9,13},{1... | collective-permute-start | bytes 786440 | tf_op jit(solution)/shard_map/ppermute | solution.py:48
  205.9 16.4 %copy-start.11 = (f32[4,4,256]{2,0,1:T(4,128)S(1)}, f32[4,4,256]{2,0,1:T(4,128)}, u32[]{:S(2)}) copy-start(f32[4,4,256]{2,0,1:T(4,128)} %copy.64) | copy-start | bytes 49156
  205.9 16.4 %copy-start.13 = (f32[128]{0:T(128)S(1)}, f32[128]{0:T(128)}, u32[]{:S(2)}) copy-start(f32[128]{0:T(128)} %add_rsqrt_fusion) | copy-start | bytes 1540
  207.9 57.3 %collective-permute-start.9 = (bf16[4,128,512]{2,1,0:T(8,128)(2,1)}, bf16[4,128,512]{2,1,0:T(8,128)(2,1)}, u32[]{:S(2)}, u32[]{:S(2)}) collective-permute-start(bf16[4,128,512]{2,1,0:T(8,128)(2,1)} %get-tuple-element.30), channel_id=1, source_target_pairs={{0,4},{1,5},{2,6},{3,7},{4,8},{5,9},{6,10},{7,11},{8,12},{9,13},{1... | collective-permute-start | bytes 1572872 | tf_op jit(solution)/shard_map/ppermute | solution.py:40
  209.8 57.3 %collective-permute-start.10 = (bf16[4,128,512]{2,1,0:T(8,128)(2,1)}, bf16[4,128,512]{2,1,0:T(8,128)(2,1)}, u32[]{:S(2)}, u32[]{:S(2)}) collective-permute-start(bf16[4,128,512]{2,1,0:T(8,128)(2,1)} %get-tuple-element.30), channel_id=1, source_target_pairs={{0,8},{1,9},{2,10},{3,11},{4,12},{5,13},{6,14},{7,15},{8,0},{9,1},... | collective-permute-start | bytes 1572872 | tf_op jit(solution)/shard_map/ppermute | solution.py:40
  213.5 53.6 %collective-permute-start.11 = (bf16[4,128,512]{2,1,0:T(8,128)(2,1)}, bf16[4,128,512]{2,1,0:T(8,128)(2,1)}, u32[]{:S(2)}, u32[]{:S(2)}) collective-permute-start(bf16[4,128,512]{2,1,0:T(8,128)(2,1)} %get-tuple-element.30), channel_id=1, source_target_pairs={{0,12},{1,13},{2,14},{3,15},{4,0},{5,1},{6,2},{7,3},{8,4},{9,5},{1... | collective-permute-start | bytes 1572872 | tf_op jit(solution)/shard_map/ppermute | solution.py:40
  219.0 12.0 %collective-permute-start.21 = (bf16[128,256]{1,0:T(8,128)(2,1)S(1)}, bf16[128,256]{1,0:T(8,128)(2,1)S(1)}, u32[]{:S(2)}, u32[]{:S(2)}) collective-permute-start(bf16[128,256]{1,0:T(8,128)(2,1)S(1)} %get-tuple-element.34), channel_id=1, source_target_pairs={{0,3},{1,0},{2,1},{3,2},{4,7},{5,4},{6,5},{7,6},{8,11},{9,8},{10,9... | collective-permute-start | bytes 196616 | tf_op jit(solution)/shard_map/ppermute | solution.py:51
  224.5 19.6 %collective-permute-start.22 = (bf16[128,256]{1,0:T(8,128)(2,1)S(1)}, bf16[128,256]{1,0:T(8,128)(2,1)S(1)}, u32[]{:S(2)}, u32[]{:S(2)}) collective-permute-start(bf16[128,256]{1,0:T(8,128)(2,1)S(1)} %get-tuple-element.36), channel_id=1, source_target_pairs={{0,2},{1,3},{2,0},{3,1},{4,6},{5,7},{6,4},{7,5},{8,10},{9,11},{10,... | collective-permute-start | bytes 196616 | tf_op jit(solution)/shard_map/ppermute | solution.py:51
  230.9 36.2 %copy-start.6 = (bf16[1,4,128,512]{3,2,1,0:T(8,128)(2,1)S(1)}, bf16[1,4,128,512]{3,2,1,0:T(8,128)(2,1)}, u32[]{:S(2)}) copy-start(bf16[1,4,128,512]{3,2,1,0:T(8,128)(2,1)} %get-tuple-element.29) | copy-start | bytes 1572868
  230.9 13.2 %collective-permute-start.23 = (bf16[128,256]{1,0:T(8,128)(2,1)S(1)}, bf16[128,256]{1,0:T(8,128)(2,1)S(1)}, u32[]{:S(2)}, u32[]{:S(2)}) collective-permute-start(bf16[128,256]{1,0:T(8,128)(2,1)S(1)} %get-tuple-element.35), channel_id=1, source_target_pairs={{0,1},{1,2},{2,3},{3,0},{4,5},{5,6},{6,7},{7,4},{8,9},{9,10},{10,1... | collective-permute-start | bytes 196616 | tf_op jit(solution)/shard_map/ppermute | solution.py:51
  245.2 49.5 %collective-permute-start.25 = (bf16[5,128,256]{2,1,0:T(8,128)(2,1)S(1)}, bf16[5,128,256]{2,1,0:T(8,128)(2,1)S(1)}, u32[]{:S(2)}, u32[]{:S(2)}) collective-permute-start(bf16[5,128,256]{2,1,0:T(8,128)(2,1)S(1)} %get-tuple-element.42), channel_id=1, source_target_pairs={{0,1},{1,2},{2,3},{3,0},{4,5},{5,6},{6,7},{7,4},{8,9},{9,10},{10,1... | collective-permute-start | bytes 983048 | tf_op jit(solution)/shard_map/ppermute | solution.py:64
  257.2 43.4 %collective-permute-start.26 = (bf16[5,128,256]{2,1,0:T(8,128)(2,1)S(1)}, bf16[5,128,256]{2,1,0:T(8,128)(2,1)S(1)}, u32[]{:S(2)}, u32[]{:S(2)}) collective-permute-start(bf16[5,128,256]{2,1,0:T(8,128)(2,1)S(1)} %get-tuple-element.43), channel_id=1, source_target_pairs={{0,2},{1,3},{2,0},{3,1},{4,6},{5,7},{6,4},{7,5},{8,10},{9,11},{10,... | collective-permute-start | bytes 983048 | tf_op jit(solution)/shard_map/ppermute | solution.py:64
  265.2 35.5 %collective-permute-start.27 = (bf16[5,128,256]{2,1,0:T(8,128)(2,1)S(1)}, bf16[5,128,256]{2,1,0:T(8,128)(2,1)S(1)}, u32[]{:S(2)}, u32[]{:S(2)}) collective-permute-start(bf16[5,128,256]{2,1,0:T(8,128)(2,1)S(1)} %get-tuple-element.44), channel_id=1, source_target_pairs={{0,3},{1,0},{2,1},{3,2},{4,7},{5,4},{6,5},{7,6},{8,11},{9,8},{10,9... | collective-permute-start | bytes 983048 | tf_op jit(solution)/shard_map/ppermute | solution.py:64
  269.7 31.3 %collective-permute-start.12 = (bf16[4,128,256]{2,1,0:T(8,128)(2,1)S(1)}, bf16[4,128,256]{2,1,0:T(8,128)(2,1)S(1)}, u32[]{:S(2)}, u32[]{:S(2)}) collective-permute-start(bf16[4,128,256]{2,1,0:T(8,128)(2,1)S(1)} %bitcast.223), channel_id=1, source_target_pairs={{0,12},{1,13},{2,14},{3,15},{4,0},{5,1},{6,2},{7,3},{8,4},{9,5},{1... | collective-permute-start | bytes 786440 | tf_op jit(solution)/shard_map/ppermute | solution.py:84
  271.6 29.4 %collective-permute-start.13 = (bf16[4,128,256]{2,1,0:T(8,128)(2,1)S(1)}, bf16[4,128,256]{2,1,0:T(8,128)(2,1)S(1)}, u32[]{:S(2)}, u32[]{:S(2)}) collective-permute-start(bf16[4,128,256]{2,1,0:T(8,128)(2,1)S(1)} %bitcast.221), channel_id=1, source_target_pairs={{0,8},{1,9},{2,10},{3,11},{4,12},{5,13},{6,14},{7,15},{8,0},{9,1},... | collective-permute-start | bytes 786440 | tf_op jit(solution)/shard_map/ppermute | solution.py:84
  294.7 11.1 %collective-permute-start.14 = (bf16[4,128,256]{2,1,0:T(8,128)(2,1)S(1)}, bf16[4,128,256]{2,1,0:T(8,128)(2,1)S(1)}, u32[]{:S(2)}, u32[]{:S(2)}) collective-permute-start(bf16[4,128,256]{2,1,0:T(8,128)(2,1)S(1)} %bitcast.219), channel_id=1, source_target_pairs={{0,4},{1,5},{2,6},{3,7},{4,8},{5,9},{6,10},{7,11},{8,12},{9,13},{1... | collective-permute-start | bytes 786440 | tf_op jit(solution)/shard_map/ppermute | solution.py:84
  306.0 36.3 %collective-permute-start.15 = (bf16[4,128,256]{2,1,0:T(8,128)(2,1)S(1)}, bf16[4,128,256]{2,1,0:T(8,128)(2,1)S(1)}, u32[]{:S(2)}, u32[]{:S(2)}) collective-permute-start(bf16[4,128,256]{2,1,0:T(8,128)(2,1)S(1)} %get-tuple-element.16), channel_id=1, source_target_pairs={{0,3},{1,0},{2,1},{3,2},{4,7},{5,4},{6,5},{7,6},{8,11},{9,8},{10,9... | collective-permute-start | bytes 786440 | tf_op jit(solution)/shard_map/ppermute | solution.py:88
  311.0 46.8 %collective-permute-start.16 = (bf16[4,128,256]{2,1,0:T(8,128)(2,1)S(1)}, bf16[4,128,256]{2,1,0:T(8,128)(2,1)S(1)}, u32[]{:S(2)}, u32[]{:S(2)}) collective-permute-start(bf16[4,128,256]{2,1,0:T(8,128)(2,1)S(1)} %get-tuple-element.18), channel_id=1, source_target_pairs={{0,2},{1,3},{2,0},{3,1},{4,6},{5,7},{6,4},{7,5},{8,10},{9,11},{10,... | collective-permute-start | bytes 786440 | tf_op jit(solution)/shard_map/ppermute | solution.py:88
  316.1 41.7 %collective-permute-start.17 = (bf16[4,128,256]{2,1,0:T(8,128)(2,1)S(1)}, bf16[4,128,256]{2,1,0:T(8,128)(2,1)S(1)}, u32[]{:S(2)}, u32[]{:S(2)}) collective-permute-start(bf16[4,128,256]{2,1,0:T(8,128)(2,1)S(1)} %get-tuple-element.15), channel_id=1, source_target_pairs={{0,1},{1,2},{2,3},{3,0},{4,5},{5,6},{6,7},{7,4},{8,9},{9,10},{10,1... | collective-permute-start | bytes 786440 | tf_op jit(solution)/shard_map/ppermute | solution.py:88
  323.5 47.4 %collective-permute-start.28 = (bf16[8,128,256]{2,1,0:T(8,128)(2,1)}, bf16[8,128,256]{2,1,0:T(8,128)(2,1)}, u32[]{:S(2)}, u32[]{:S(2)}) collective-permute-start(bf16[8,128,256]{2,1,0:T(8,128)(2,1)} %get-tuple-element.31), channel_id=1, source_target_pairs={{0,4},{1,5},{2,6},{3,7},{4,8},{5,9},{6,10},{7,11},{8,12},{9,13},{1... | collective-permute-start | bytes 1572872 | tf_op jit(solution)/shard_map/ppermute | solution.py:71
  329.7 42.4 %collective-permute-start.29 = (bf16[8,128,256]{2,1,0:T(8,128)(2,1)}, bf16[8,128,256]{2,1,0:T(8,128)(2,1)}, u32[]{:S(2)}, u32[]{:S(2)}) collective-permute-start(bf16[8,128,256]{2,1,0:T(8,128)(2,1)} %get-tuple-element.32), channel_id=1, source_target_pairs={{0,8},{1,9},{2,10},{3,11},{4,12},{5,13},{6,14},{7,15},{8,0},{9,1},... | collective-permute-start | bytes 1572872 | tf_op jit(solution)/shard_map/ppermute | solution.py:71
  342.3 30.8 %collective-permute-start.30 = (bf16[8,128,256]{2,1,0:T(8,128)(2,1)}, bf16[8,128,256]{2,1,0:T(8,128)(2,1)}, u32[]{:S(2)}, u32[]{:S(2)}) collective-permute-start(bf16[8,128,256]{2,1,0:T(8,128)(2,1)} %get-tuple-element.33), channel_id=1, source_target_pairs={{0,12},{1,13},{2,14},{3,15},{4,0},{5,1},{6,2},{7,3},{8,4},{9,5},{1... | collective-permute-start | bytes 1572872 | tf_op jit(solution)/shard_map/ppermute | solution.py:71
  362.8 3.3 copy-start.4
  366.8 63.2 %collective-permute-start.24 = (bf16[128,4096]{1,0:T(8,128)(2,1)S(1)}, bf16[128,4096]{1,0:T(8,128)(2,1)S(1)}, u32[]{:S(2)}, u32[]{:S(2)}) collective-permute-start(bf16[128,4096]{1,0:T(8,128)(2,1)S(1)} %add_convert_fusion), channel_id=1, source_target_pairs={{0,16},{16,32},{32,48},{48,64},{64,80},{80,96},{96,112},{112,128},... | collective-permute-start | bytes 3145736 | tf_op jit(solution)/shard_map/ppermute | solution.py:14
  374.4 54.7 %copy-start.8 = (bf16[1,256,768]{2,1,0:T(8,128)(2,1)S(1)}, bf16[1,256,768]{2,1,0:T(8,128)(2,1)}, u32[]{:S(2)}) copy-start(bf16[1,256,768]{2,1,0:T(8,128)(2,1)} %param.14) | copy-start | bytes 1179652
  376.8 52.3 %collective-permute-start.31 = (bf16[256,768]{1,0:T(8,128)(2,1)S(1)}, bf16[256,768]{1,0:T(8,128)(2,1)S(1)}, u32[]{:S(2)}, u32[]{:S(2)}) collective-permute-start(bf16[256,768]{1,0:T(8,128)(2,1)S(1)} %fusion.35), channel_id=1, source_target_pairs={{0,496},{16,480},{32,464},{48,448},{64,432},{80,416},{96,400},{112... | collective-permute-start | bytes 1179656 | tf_op jit(solution)/shard_map/ppermute | solution.py:19
  (4 other events, 8.6 us)
Sparse Core Ops, SparseCore 0:
  11.0 133.4 all-gather.5
  147.5 135.8 all-gather.3
where the time goes:
time: 439 us; the launch traced here: 438 us
  starting transfers between devices  188 us (43%)
  waiting for transfers between devices  161 us (37%)
  matrix products  32.7 us (7%)
  local copies, waits for them, and re-layouts  22.6 us (5%)
  other arithmetic  18.5 us (4%)
  between operations  15.1 us (3%)
    all_gather x1, waiting for transfers between devices, per_device(): lax.all_gather(up_output_weight[0], 'seq', axis=1, tiled=True)  80.2 us
    ppermute x6, starting transfers between devices, gather_blocks(): lax.ppermute(x, 'seq', seq_pairs(k, 0))  40.2 us
    ppermute x1, starting transfers between devices, mirrored(): lax.ppermute(value, axis, [(source, count - 1 - source) for source in ran...  34.8 us
    ppermute x3, starting transfers between devices, gather_and_scatter(): lax.ppermute(jnp.concatenate([x, piece]), 'seq', seq_pairs(k, 0))  21.9 us
    ppermute x3, waiting for transfers between devices, gather_columns(): second.append(lax.ppermute(first[k], 'seq', seq_pairs(INNER - k, 0)))  20.5 us
    ppermute x6, starting transfers between devices, gather_blocks(): lax.ppermute(first, 'seq', seq_pairs(k, 1))  18.4 us
    ppermute x3, waiting for transfers between devices, gather_and_scatter(): lax.ppermute(jnp.concatenate([x, piece]), 'seq', seq_pairs(k, 0))  17.4 us
    ppermute x1, waiting for transfers between devices, mirrored(): lax.ppermute(value, axis, [(source, count - 1 - source) for source in ran...  17.4 us
  transfers between devices with their start and end apart: 34, of which 10 were waited for; matrix products, arithmetic and copies ran while one was open for 16% of the time, Pallas kernels for 0%

commit v1 on v0

--- a/solution.py
+++ b/solution.py
@@ -6,6 +6,16 @@
 HEAD = 128
 GROUP = 4
 INNER = 4
+
+
+def sheet_work(array_in, peer_axis, dimension_no):
+    spare = lax.all_to_all(
+        jnp.stack([array_in for _ in range(lax.axis_size(peer_axis))], 0),
+        axis_name=peer_axis,
+        split_axis=0,
+        concat_axis=0,
+    )
+    return jnp.concatenate(spare, dimension_no)
 
 
 def shifted(value, axis, steps):
@@ -132,7 +142,7 @@
     cotangent = up_cotangent[0]
     unit_up, inverse_up, normed_up = normalize(up_activation[0], upward_gain[0])
     hidden = normed_up.astype(jnp.bfloat16)
-    output_weight = lax.all_gather(up_output_weight[0], "seq", axis=1, tiled=True)
+    output_weight = sheet_work(up_output_weight[0], "seq", 1)
     key_value = gather_blocks(saved[:, width:]).reshape(size * count, 2 * HEAD)
     kv_weight_all = lax.all_gather(up_input_weight[0][:, width:], "seq", axis=0, tiled=True)
     keys = key_value[:, :HEAD]

time: 439 us -> 577 us (1.31)
  the two profiles are of different devices: /device:TPU:43 before, /device:TPU:68 now
where the time goes in v1:
time: 577 us; the launch traced here: 575 us
  waiting for transfers between devices  312 us (54%)
  starting transfers between devices  159 us (28%)
  matrix products  36.2 us (6%)
  local copies, waits for them, and re-layouts  28.1 us (5%)
  other arithmetic  23.8 us (4%)
  between operations  15 us (3%)
    ppermute x6, waiting for transfers between devices, gather_blocks(): lax.ppermute(x, 'seq', seq_pairs(k, 0))  222 us
    ppermute x6, starting transfers between devices, gather_blocks(): lax.ppermute(x, 'seq', seq_pairs(k, 0))  38.4 us
    ppermute x6, waiting for transfers between devices, gather_blocks(): lax.ppermute(first, 'seq', seq_pairs(k, 1))  27.9 us
    ppermute x1, waiting for transfers between devices, mirrored(): lax.ppermute(value, axis, [(source, count - 1 - source) for source in ran...  24.9 us
    ppermute x6, starting transfers between devices, gather_blocks(): lax.ppermute(first, 'seq', seq_pairs(k, 1))  18.2 us
    ppermute x3, starting transfers between devices, gather_and_scatter(): lax.ppermute(jnp.concatenate([x, piece]), 'seq', seq_pairs(k, 0))  17.8 us
    ppermute x3, starting transfers between devices, gather_columns(): second.append(lax.ppermute(first[k], 'seq', seq_pairs(INNER - k, 0)))  16.9 us
    all_to_all x1, starting transfers between devices, sheet_work(): lax.all_to_all(jnp.stack([array_in for _ in range(lax.axis_size(peer_axis...  16.4 us
  transfers between devices with their start and end apart: 34, of which 17 were waited for; matrix products, arithmetic and copies ran while one was open for 14% of the time, Pallas kernels for 0%

profile of v1, /device:TPU:68, one launch (start us, length us, event | category | flops | bytes accessed | tf_op | source)
XLA Modules:
  0.0 574.9 jit_solution(3548034808544211371)
XLA Ops:
  10.7 16.4 %all-to-all-start = ((bf16[16,512,256]{1,2,0:T(8,128)(2,1)}), bf16[16,512,256]{1,2,0:T(8,128)(2,1)}, u32[]{:S(2)}, u32[]{:S(2)}) async-start(bf16[16,512,256]{1,2,0:T(8,128)(2,1)} %stack.128), calls=%async_computation | async-start | bytes 8388608 | tf_op jit(solution)/shard_map/all_to_all | solution.py:12
  27.3 7.4 %collective-permute-start = (bf16[128,256]{0,1:T(8,128)(2,1)S(1)}, bf16[128,256]{0,1:T(8,128)(2,1)S(1)}, u32[]{:S(2)}, u32[]{:S(2)}) collective-permute-start(bf16[128,256]{0,1:T(8,128)(2,1)S(1)} %get-tuple-element.40), channel_id=1, source_target_pairs={{0,1},{1,2},{2,3},{3,0},{4,5},{5,6},{6,7},{7,4},{8,9},{9,10},{10,1... | collective-permute-start | bytes 196616 | tf_op jit(solution)/shard_map/ppermute | solution.py:48
  34.8 7.3 %collective-permute-start.1 = (bf16[128,256]{0,1:T(8,128)(2,1)S(1)}, bf16[128,256]{0,1:T(8,128)(2,1)S(1)}, u32[]{:S(2)}, u32[]{:S(2)}) collective-permute-start(bf16[128,256]{0,1:T(8,128)(2,1)S(1)} %get-tuple-element.40), channel_id=1, source_target_pairs={{0,2},{1,3},{2,0},{3,1},{4,6},{5,7},{6,4},{7,5},{8,10},{9,11},{10,... | collective-permute-start | bytes 196616 | tf_op jit(solution)/shard_map/ppermute | solution.py:48
  42.0 7.3 %collective-permute-start.2 = (bf16[128,256]{0,1:T(8,128)(2,1)S(1)}, bf16[128,256]{0,1:T(8,128)(2,1)S(1)}, u32[]{:S(2)}, u32[]{:S(2)}) collective-permute-start(bf16[128,256]{0,1:T(8,128)(2,1)S(1)} %get-tuple-element.40), channel_id=1, source_target_pairs={{0,3},{1,0},{2,1},{3,2},{4,7},{5,4},{6,5},{7,6},{8,11},{9,8},{10,9... | collective-permute-start | bytes 196616 | tf_op jit(solution)/shard_map/ppermute | solution.py:48
  52.3 175.7 %collective-permute-done = bf16[128,256]{0,1:T(8,128)(2,1)S(1)} collective-permute-done((bf16[128,256]{0,1:T(8,128)(2,1)S(1)}, bf16[128,256]{0,1:T(8,128)(2,1)S(1)}, u32[]{:S(2)}, u32[]{:S(2)}) %collective-permute-start) | collective-permute-done | bytes 65568 | tf_op jit(solution)/shard_map/ppermute | solution.py:48
  228.0 7.9 %collective-permute-done.1 = bf16[128,256]{0,1:T(8,128)(2,1)S(1)} collective-permute-done((bf16[128,256]{0,1:T(8,128)(2,1)S(1)}, bf16[128,256]{0,1:T(8,128)(2,1)S(1)}, u32[]{:S(2)}, u32[]{:S(2)}) %collective-permute-start.1) | collective-permute-done | bytes 65568 | tf_op jit(solution)/shard_map/ppermute | solution.py:48
  236.6 5.2 collective-permute-start.3
  241.8 3.0 collective-permute-start.4
  255.4 3.0 collective-permute-done.4
  265.3 5.4 fusion.83
  270.7 3.3 convolution_convert_fusion.1
  274.2 3.9 fusion.59
  279.8 8.3 %convolution_bitcast_fusion.1 = f32[2048,128]{0,1:T(8,128)} fusion(bf16[128,4,128]{0,2,1:T(8,128)(2,1)S(1)} %bitcast.227, f32[128,4,2048]{0,2,1:T(8,128)} %fusion.59, f32[128,4,2048]{0,2,1:T(8,128)} %get-tuple-element.46, f32[128,4]{0,1:T(4,128)S(1)} %copy-done.21), kind=kOutput, calls=%fused_computation.25 | convolution fusion | flops 275778048 | bytes 9570304 | tf_op jit(solution)/shard_map/tgj,tgh->jh/dot_general | solution.py:179
  292.4 2.9 collective-permute-start.18
  297.1 3.7 collective-permute-start.19
  307.4 2.7 collective-permute-done.19
  310.1 3.9 collective-permute-done.20
  315.1 6.7 %collective-permute-start.21 = (bf16[128,256]{1,0:T(8,128)(2,1)S(1)}, bf16[128,256]{1,0:T(8,128)(2,1)S(1)}, u32[]{:S(2)}, u32[]{:S(2)}) collective-permute-start(bf16[128,256]{1,0:T(8,128)(2,1)S(1)} %get-tuple-element.34), channel_id=1, source_target_pairs={{0,3},{1,0},{2,1},{3,2},{4,7},{5,4},{6,5},{7,6},{8,11},{9,8},{10,9... | collective-permute-start | bytes 196616 | tf_op jit(solution)/shard_map/ppermute | solution.py:61
  321.8 2.7 collective-permute-start.22
  324.5 6.7 %collective-permute-start.23 = (bf16[128,256]{1,0:T(8,128)(2,1)S(1)}, bf16[128,256]{1,0:T(8,128)(2,1)S(1)}, u32[]{:S(2)}, u32[]{:S(2)}) collective-permute-start(bf16[128,256]{1,0:T(8,128)(2,1)S(1)} %get-tuple-element.35), channel_id=1, source_target_pairs={{0,1},{1,2},{2,3},{3,0},{4,5},{5,6},{6,7},{7,4},{8,9},{9,10},{10,1... | collective-permute-start | bytes 196616 | tf_op jit(solution)/shard_map/ppermute | solution.py:61
  331.3 13.3 %collective-permute-done.22 = bf16[128,256]{1,0:T(8,128)(2,1)S(1)} collective-permute-done((bf16[128,256]{1,0:T(8,128)(2,1)S(1)}, bf16[128,256]{1,0:T(8,128)(2,1)S(1)}, u32[]{:S(2)}, u32[]{:S(2)}) %collective-permute-start.22) | collective-permute-done | bytes 65568 | tf_op jit(solution)/shard_map/ppermute | solution.py:61
  345.9 6.7 %collective-permute-start.25 = (bf16[5,128,256]{2,1,0:T(8,128)(2,1)}, bf16[5,128,256]{2,1,0:T(8,128)(2,1)S(1)}, u32[]{:S(2)}, u32[]{:S(2)}) collective-permute-start(bf16[5,128,256]{2,1,0:T(8,128)(2,1)} %get-tuple-element.42), channel_id=1, source_target_pairs={{0,1},{1,2},{2,3},{3,0},{4,5},{5,6},{6,7},{7,4},{8,9},{9,10},{10,1... | collective-permute-start | bytes 983048 | tf_op jit(solution)/shard_map/ppermute | solution.py:74
  352.6 7.2 %fusion.36 = bf16[128,4,128]{0,2,1:T(8,128)(2,1)S(1)} fusion(f32[128,4,2048]{0,2,1:T(8,128)} %fusion.59, bf16[2048,256]{1,0:T(8,128)(2,1)S(1)} %bitcast.196, f32[128,4,2048]{0,2,1:T(8,128)} %get-tuple-element.46, f32[128,4]{0,1:T(4,128)} %get-tuple-element.45), kind=kOutput, calls=%fused_computation.57 | convolution fusion | flops 275843584 | bytes 17436672 | tf_op jit(solution)/shard_map/tgj,jh->tgh/dot_general | solution.py:175
  359.9 3.0 collective-permute-start.6
  362.9 7.5 %collective-permute-start.7 = (bf16[128,512]{1,0:T(8,128)(2,1)S(1)}, bf16[128,512]{1,0:T(8,128)(2,1)S(1)}, u32[]{:S(2)}, u32[]{:S(2)}) collective-permute-start(bf16[128,512]{1,0:T(8,128)(2,1)S(1)} %copy.49), channel_id=1, source_target_pairs={{0,2},{1,3},{2,0},{3,1},{4,6},{5,7},{6,4},{7,5},{8,10},{9,11},{10,... | collective-permute-start | bytes 393224 | tf_op jit(solution)/shard_map/ppermute | solution.py:48
  370.5 5.9 %collective-permute-start.8 = (bf16[128,512]{1,0:T(8,128)(2,1)S(1)}, bf16[128,512]{1,0:T(8,128)(2,1)S(1)}, u32[]{:S(2)}, u32[]{:S(2)}) collective-permute-start(bf16[128,512]{1,0:T(8,128)(2,1)S(1)} %copy.49), channel_id=1, source_target_pairs={{0,3},{1,0},{2,1},{3,2},{4,7},{5,4},{6,5},{7,6},{8,11},{9,8},{10,9... | collective-permute-start | bytes 393224 | tf_op jit(solution)/shard_map/ppermute | solution.py:48
  376.4 7.9 %collective-permute-start.26 = (bf16[5,128,256]{2,1,0:T(8,128)(2,1)}, bf16[5,128,256]{2,1,0:T(8,128)(2,1)S(1)}, u32[]{:S(2)}, u32[]{:S(2)}) collective-permute-start(bf16[5,128,256]{2,1,0:T(8,128)(2,1)} %get-tuple-element.43), channel_id=1, source_target_pairs={{0,2},{1,3},{2,0},{3,1},{4,6},{5,7},{6,4},{7,5},{8,10},{9,11},{10,... | collective-permute-start | bytes 983048 | tf_op jit(solution)/shard_map/ppermute | solution.py:74
  384.3 3.2 collective-permute-start.27
  387.7 38.2 %collective-permute-done.8 = bf16[128,512]{1,0:T(8,128)(2,1)S(1)} collective-permute-done((bf16[128,512]{1,0:T(8,128)(2,1)S(1)}, bf16[128,512]{1,0:T(8,128)(2,1)S(1)}, u32[]{:S(2)}, u32[]{:S(2)}) %collective-permute-start.8) | collective-permute-done | bytes 131104 | tf_op jit(solution)/shard_map/ppermute | solution.py:48
  430.2 3.3 collective-permute-start.10
  433.5 2.5 collective-permute-start.11
  436.5 18.8 %collective-permute-done.9 = bf16[4,128,512]{2,1,0:T(8,128)(2,1)} collective-permute-done((bf16[4,128,512]{2,1,0:T(8,128)(2,1)}, bf16[4,128,512]{2,1,0:T(8,128)(2,1)}, u32[]{:S(2)}, u32[]{:S(2)}) %collective-permute-start.9) | collective-permute-done | bytes 524320 | tf_op jit(solution)/shard_map/ppermute | solution.py:50
  455.4 3.7 collective-permute-done.11
  462.4 3.3 collective-permute-start.12
  465.8 2.8 collective-permute-start.13
  468.6 3.1 collective-permute-start.14
  471.8 4.5 collective-permute-start.28
  478.3 3.5 collective-permute-start.30
  484.5 4.4 collective-permute-start.15
  488.9 8.8 %collective-permute-start.16 = (bf16[4,128,256]{2,1,0:T(8,128)(2,1)S(1)}, bf16[4,128,256]{2,1,0:T(8,128)(2,1)S(1)}, u32[]{:S(2)}, u32[]{:S(2)}) collective-permute-start(bf16[4,128,256]{2,1,0:T(8,128)(2,1)S(1)} %get-tuple-element.18), channel_id=1, source_target_pairs={{0,2},{1,3},{2,0},{3,1},{4,6},{5,7},{6,4},{7,5},{8,10},{9,11},{10,... | collective-permute-start | bytes 786440 | tf_op jit(solution)/shard_map/ppermute | solution.py:98
  497.7 3.7 collective-permute-start.17
  508.0 3.5 collective-permute-done.15
  511.6 8.2 %collective-permute-done.16 = bf16[4,128,256]{2,1,0:T(8,128)(2,1)S(1)} collective-permute-done((bf16[4,128,256]{2,1,0:T(8,128)(2,1)S(1)}, bf16[4,128,256]{2,1,0:T(8,128)(2,1)S(1)}, u32[]{:S(2)}, u32[]{:S(2)}) %collective-permute-start.16) | collective-permute-done | bytes 262176 | tf_op jit(solution)/shard_map/ppermute | solution.py:98
  519.8 2.4 collective-permute-done.17
  527.2 3.2 multiply_reduce_fusion.1
  533.2 2.4 fusion.33
  535.6 5.8 %collective-permute-start.31 = (bf16[256,768]{1,0:T(8,128)(2,1)S(1)}, bf16[256,768]{1,0:T(8,128)(2,1)S(1)}, u32[]{:S(2)}, u32[]{:S(2)}) collective-permute-start(bf16[256,768]{1,0:T(8,128)(2,1)S(1)} %fusion.33), channel_id=1, source_target_pairs={{0,496},{16,480},{32,464},{48,448},{64,432},{80,416},{96,400},{112... | collective-permute-start | bytes 1179656 | tf_op jit(solution)/shard_map/ppermute | solution.py:29
  541.4 24.9 %collective-permute-done.31 = bf16[256,768]{1,0:T(8,128)(2,1)S(1)} collective-permute-done((bf16[256,768]{1,0:T(8,128)(2,1)S(1)}, bf16[256,768]{1,0:T(8,128)(2,1)S(1)}, u32[]{:S(2)}, u32[]{:S(2)}) %collective-permute-start.31) | collective-permute-done | bytes 393248 | tf_op jit(solution)/shard_map/ppermute | solution.py:29
  (134 shorter events, 71.0 us)
Async XLA Ops:
  10.7 16.5 %copy-start.12 = (bf16[1,128,768]{2,1,0:T(8,128)(2,1)S(1)}, bf16[1,128,768]{2,1,0:T(8,128)(2,1)}, u32[]{:S(2)}) copy-start(bf16[1,128,768]{2,1,0:T(8,128)(2,1)} %param.9) | copy-start | bytes 589828
  10.7 40.5 %copy-start.19 = (s32[1,128]{1,0:T(1,128)S(1)}, s32[1,128]{1,0:T(1,128)}, u32[]{:S(2)}) copy-start(s32[1,128]{1,0:T(1,128)} %param.15) | copy-start | bytes 1540
  10.7 260.1 %all-to-all-start = ((bf16[16,512,256]{1,2,0:T(8,128)(2,1)}), bf16[16,512,256]{1,2,0:T(8,128)(2,1)}, u32[]{:S(2)}, u32[]{:S(2)}) async-start(bf16[16,512,256]{1,2,0:T(8,128)(2,1)} %stack.128), calls=%async_computation | async-start | bytes 8388608 | tf_op jit(solution)/shard_map/all_to_all | solution.py:12
  27.1 220.0 %copy-start = (bf16[1,128,4096]{2,1,0:T(8,128)(2,1)S(1)}, bf16[1,128,4096]{2,1,0:T(8,128)(2,1)}, u32[]{:S(2)}) copy-start(bf16[1,128,4096]{2,1,0:T(8,128)(2,1)} %param.8) | copy-start | bytes 3145732
  27.1 500.1 %all-gather.2.cloned.1.call-start = ((), (), s32[]{:S(2)}) async-start(), calls=%async_computation.1 | async-start | bytes 2228224 | tf_op jit(solution)/shard_map/all_gather | solution.py:147
  27.3 200.6 %collective-permute-start = (bf16[128,256]{0,1:T(8,128)(2,1)S(1)}, bf16[128,256]{0,1:T(8,128)(2,1)S(1)}, u32[]{:S(2)}, u32[]{:S(2)}) collective-permute-start(bf16[128,256]{0,1:T(8,128)(2,1)S(1)} %get-tuple-element.40), channel_id=1, source_target_pairs={{0,1},{1,2},{2,3},{3,0},{4,5},{5,6},{6,7},{7,4},{8,9},{9,10},{10,1... | collective-permute-start | bytes 196616 | tf_op jit(solution)/shard_map/ppermute | solution.py:48
  34.8 201.1 %collective-permute-start.1 = (bf16[128,256]{0,1:T(8,128)(2,1)S(1)}, bf16[128,256]{0,1:T(8,128)(2,1)S(1)}, u32[]{:S(2)}, u32[]{:S(2)}) collective-permute-start(bf16[128,256]{0,1:T(8,128)(2,1)S(1)} %get-tuple-element.40), channel_id=1, source_target_pairs={{0,2},{1,3},{2,0},{3,1},{4,6},{5,7},{6,4},{7,5},{8,10},{9,11},{10,... | collective-permute-start | bytes 196616 | tf_op jit(solution)/shard_map/ppermute | solution.py:48
  42.0 193.8 %collective-permute-start.2 = (bf16[128,256]{0,1:T(8,128)(2,1)S(1)}, bf16[128,256]{0,1:T(8,128)(2,1)S(1)}, u32[]{:S(2)}, u32[]{:S(2)}) collective-permute-start(bf16[128,256]{0,1:T(8,128)(2,1)S(1)} %get-tuple-element.40), channel_id=1, source_target_pairs={{0,3},{1,0},{2,1},{3,2},{4,7},{5,4},{6,5},{7,6},{8,11},{9,8},{10,9... | collective-permute-start | bytes 196616 | tf_op jit(solution)/shard_map/ppermute | solution.py:48
  236.6 13.7 %copy-start.14 = (f32[1,4096]{1,0:T(1,128)S(1)}, f32[1,4096]{1,0:T(1,128)}, u32[]{:S(2)}) copy-start(f32[1,4096]{1,0:T(1,128)} %param.13) | copy-start | bytes 49156
  236.6 18.8 %collective-permute-start.3 = (bf16[4,128,256]{1,2,0:T(8,128)(2,1)}, bf16[4,128,256]{1,2,0:T(8,128)(2,1)}, u32[]{:S(2)}, u32[]{:S(2)}) collective-permute-start(bf16[4,128,256]{1,2,0:T(8,128)(2,1)} %get-tuple-element.38), channel_id=1, source_target_pairs={{0,4},{1,5},{2,6},{3,7},{4,8},{5,9},{6,10},{7,11},{8,12},{9,13},{1... | collective-permute-start | bytes 786440 | tf_op jit(solution)/shard_map/ppermute | solution.py:50
  241.8 16.7 %collective-permute-start.4 = (bf16[4,128,256]{1,2,0:T(8,128)(2,1)}, bf16[4,128,256]{1,2,0:T(8,128)(2,1)}, u32[]{:S(2)}, u32[]{:S(2)}) collective-permute-start(bf16[4,128,256]{1,2,0:T(8,128)(2,1)} %get-tuple-element.38), channel_id=1, source_target_pairs={{0,8},{1,9},{2,10},{3,11},{4,12},{5,13},{6,14},{7,15},{8,0},{9,1},... | collective-permute-start | bytes 786440 | tf_op jit(solution)/shard_map/ppermute | solution.py:50
  244.8 16.0 %collective-permute-start.5 = (bf16[4,128,256]{1,2,0:T(8,128)(2,1)}, bf16[4,128,256]{1,2,0:T(8,128)(2,1)}, u32[]{:S(2)}, u32[]{:S(2)}) collective-permute-start(bf16[4,128,256]{1,2,0:T(8,128)(2,1)} %get-tuple-element.38), channel_id=1, source_target_pairs={{0,12},{1,13},{2,14},{3,15},{4,0},{5,1},{6,2},{7,3},{8,4},{9,5},{1... | collective-permute-start | bytes 786440 | tf_op jit(solution)/shard_map/ppermute | solution.py:50
  274.1 3.9 copy-start.20
  274.1 3.9 copy-start.21
  289.8 14.1 %copy-start.15 = (f32[4,4,256]{2,0,1:T(4,128)S(1)}, f32[4,4,256]{2,0,1:T(4,128)}, u32[]{:S(2)}) copy-start(f32[4,4,256]{2,0,1:T(4,128)} %copy.65) | copy-start | bytes 49156
  289.8 14.1 %copy-start.17 = (f32[128]{0:T(128)S(1)}, f32[128]{0:T(128)}, u32[]{:S(2)}) copy-start(f32[128]{0:T(128)} %add_rsqrt_fusion) | copy-start | bytes 1540
  292.4 15.0 %collective-permute-start.18 = (bf16[4,128,256]{2,1,0:T(8,128)(2,1)}, bf16[4,128,256]{2,1,0:T(8,128)(2,1)}, u32[]{:S(2)}, u32[]{:S(2)}) collective-permute-start(bf16[4,128,256]{2,1,0:T(8,128)(2,1)} %bitcast.220), channel_id=1, source_target_pairs={{0,12},{1,13},{2,14},{3,15},{4,0},{5,1},{6,2},{7,3},{8,4},{9,5},{1... | collective-permute-start | bytes 786440 | tf_op jit(solution)/shard_map/ppermute | solution.py:58
  297.1 12.9 %collective-permute-start.19 = (bf16[4,128,256]{2,1,0:T(8,128)(2,1)}, bf16[4,128,256]{2,1,0:T(8,128)(2,1)}, u32[]{:S(2)}, u32[]{:S(2)}) collective-permute-start(bf16[4,128,256]{2,1,0:T(8,128)(2,1)} %bitcast.221), channel_id=1, source_target_pairs={{0,8},{1,9},{2,10},{3,11},{4,12},{5,13},{6,14},{7,15},{8,0},{9,1},... | collective-permute-start | bytes 786440 | tf_op jit(solution)/shard_map/ppermute | solution.py:58
  301.7 12.3 %collective-permute-start.20 = (bf16[4,128,256]{2,1,0:T(8,128)(2,1)}, bf16[4,128,256]{2,1,0:T(8,128)(2,1)S(1)}, u32[]{:S(2)}, u32[]{:S(2)}) collective-permute-start(bf16[4,128,256]{2,1,0:T(8,128)(2,1)} %bitcast.222), channel_id=1, source_target_pairs={{0,4},{1,5},{2,6},{3,7},{4,8},{5,9},{6,10},{7,11},{8,12},{9,13},{1... | collective-permute-start | bytes 786440 | tf_op jit(solution)/shard_map/ppermute | solution.py:58
  307.2 24.0 %copy-start.1 = (bf16[128,4,4,256]{3,0,1,2:T(8,128)(2,1)S(1)}, bf16[128,4,4,256]{3,0,1,2:T(8,128)(2,1)}, u32[]{:S(2)}) copy-start(bf16[128,4,4,256]{3,0,1,2:T(8,128)(2,1)} %fusion.20) | copy-start | bytes 3145732
  315.1 16.1 %collective-permute-start.21 = (bf16[128,256]{1,0:T(8,128)(2,1)S(1)}, bf16[128,256]{1,0:T(8,128)(2,1)S(1)}, u32[]{:S(2)}, u32[]{:S(2)}) collective-permute-start(bf16[128,256]{1,0:T(8,128)(2,1)S(1)} %get-tuple-element.34), channel_id=1, source_target_pairs={{0,3},{1,0},{2,1},{3,2},{4,7},{5,4},{6,5},{7,6},{8,11},{9,8},{10,9... | collective-permute-start | bytes 196616 | tf_op jit(solution)/shard_map/ppermute | solution.py:61
  321.8 22.8 %collective-permute-start.22 = (bf16[128,256]{1,0:T(8,128)(2,1)S(1)}, bf16[128,256]{1,0:T(8,128)(2,1)S(1)}, u32[]{:S(2)}, u32[]{:S(2)}) collective-permute-start(bf16[128,256]{1,0:T(8,128)(2,1)S(1)} %get-tuple-element.36), channel_id=1, source_target_pairs={{0,2},{1,3},{2,0},{3,1},{4,6},{5,7},{6,4},{7,5},{8,10},{9,11},{10,... | collective-permute-start | bytes 196616 | tf_op jit(solution)/shard_map/ppermute | solution.py:61
  324.4 28.1 %copy-start.3 = (bf16[4,4,128,256]{3,2,1,0:T(8,128)(2,1)S(1)}, bf16[4,4,128,256]{3,2,1,0:T(8,128)(2,1)}, u32[]{:S(2)}) copy-start(bf16[4,4,128,256]{3,2,1,0:T(8,128)(2,1)} %copy.41) | copy-start | bytes 3145732
  324.5 20.4 %collective-permute-start.23 = (bf16[128,256]{1,0:T(8,128)(2,1)S(1)}, bf16[128,256]{1,0:T(8,128)(2,1)S(1)}, u32[]{:S(2)}, u32[]{:S(2)}) collective-permute-start(bf16[128,256]{1,0:T(8,128)(2,1)S(1)} %get-tuple-element.35), channel_id=1, source_target_pairs={{0,1},{1,2},{2,3},{3,0},{4,5},{5,6},{6,7},{7,4},{8,9},{9,10},{10,1... | collective-permute-start | bytes 196616 | tf_op jit(solution)/shard_map/ppermute | solution.py:61
  345.9 87.6 %collective-permute-start.25 = (bf16[5,128,256]{2,1,0:T(8,128)(2,1)}, bf16[5,128,256]{2,1,0:T(8,128)(2,1)S(1)}, u32[]{:S(2)}, u32[]{:S(2)}) collective-permute-start(bf16[5,128,256]{2,1,0:T(8,128)(2,1)} %get-tuple-element.42), channel_id=1, source_target_pairs={{0,1},{1,2},{2,3},{3,0},{4,5},{5,6},{6,7},{7,4},{8,9},{9,10},{10,1... | collective-permute-start | bytes 983048 | tf_op jit(solution)/shard_map/ppermute | solution.py:74
  359.9 24.3 %collective-permute-start.6 = (bf16[128,512]{1,0:T(8,128)(2,1)S(1)}, bf16[128,512]{1,0:T(8,128)(2,1)S(1)}, u32[]{:S(2)}, u32[]{:S(2)}) collective-permute-start(bf16[128,512]{1,0:T(8,128)(2,1)S(1)} %copy.49), channel_id=1, source_target_pairs={{0,1},{1,2},{2,3},{3,0},{4,5},{5,6},{6,7},{7,4},{8,9},{9,10},{10,1... | collective-permute-start | bytes 393224 | tf_op jit(solution)/shard_map/ppermute | solution.py:48
  362.9 24.7 %collective-permute-start.7 = (bf16[128,512]{1,0:T(8,128)(2,1)S(1)}, bf16[128,512]{1,0:T(8,128)(2,1)S(1)}, u32[]{:S(2)}, u32[]{:S(2)}) collective-permute-start(bf16[128,512]{1,0:T(8,128)(2,1)S(1)} %copy.49), channel_id=1, source_target_pairs={{0,2},{1,3},{2,0},{3,1},{4,6},{5,7},{6,4},{7,5},{8,10},{9,11},{10,... | collective-permute-start | bytes 393224 | tf_op jit(solution)/shard_map/ppermute | solution.py:48
  370.5 55.4 %collective-permute-start.8 = (bf16[128,512]{1,0:T(8,128)(2,1)S(1)}, bf16[128,512]{1,0:T(8,128)(2,1)S(1)}, u32[]{:S(2)}, u32[]{:S(2)}) collective-permute-start(bf16[128,512]{1,0:T(8,128)(2,1)S(1)} %copy.49), channel_id=1, source_target_pairs={{0,3},{1,0},{2,1},{3,2},{4,7},{5,4},{6,5},{7,6},{8,11},{9,8},{10,9... | collective-permute-start | bytes 393224 | tf_op jit(solution)/shard_map/ppermute | solution.py:48
  376.4 59.7 %collective-permute-start.26 = (bf16[5,128,256]{2,1,0:T(8,128)(2,1)}, bf16[5,128,256]{2,1,0:T(8,128)(2,1)S(1)}, u32[]{:S(2)}, u32[]{:S(2)}) collective-permute-start(bf16[5,128,256]{2,1,0:T(8,128)(2,1)} %get-tuple-element.43), channel_id=1, source_target_pairs={{0,2},{1,3},{2,0},{3,1},{4,6},{5,7},{6,4},{7,5},{8,10},{9,11},{10,... | collective-permute-start | bytes 983048 | tf_op jit(solution)/shard_map/ppermute | solution.py:74
  384.3 51.9 %collective-permute-start.27 = (bf16[5,128,256]{2,1,0:T(8,128)(2,1)}, bf16[5,128,256]{2,1,0:T(8,128)(2,1)S(1)}, u32[]{:S(2)}, u32[]{:S(2)}) collective-permute-start(bf16[5,128,256]{2,1,0:T(8,128)(2,1)} %get-tuple-element.44), channel_id=1, source_target_pairs={{0,3},{1,0},{2,1},{3,2},{4,7},{5,4},{6,5},{7,6},{8,11},{9,8},{10,9... | collective-permute-start | bytes 983048 | tf_op jit(solution)/shard_map/ppermute | solution.py:74
  428.3 30.8 %copy-start.4 = (bf16[1,4,128,512]{3,2,1,0:T(8,128)(2,1)}, bf16[1,4,128,512]{3,2,1,0:T(8,128)(2,1)S(1)}, u32[]{:S(2)}) copy-start(bf16[1,4,128,512]{3,2,1,0:T(8,128)(2,1)S(1)} %get-tuple-element.29) | copy-start | bytes 1572868
  428.3 27.1 %collective-permute-start.9 = (bf16[4,128,512]{2,1,0:T(8,128)(2,1)}, bf16[4,128,512]{2,1,0:T(8,128)(2,1)}, u32[]{:S(2)}, u32[]{:S(2)}) collective-permute-start(bf16[4,128,512]{2,1,0:T(8,128)(2,1)} %get-tuple-element.30), channel_id=1, source_target_pairs={{0,4},{1,5},{2,6},{3,7},{4,8},{5,9},{6,10},{7,11},{8,12},{9,13},{1... | collective-permute-start | bytes 1572872 | tf_op jit(solution)/shard_map/ppermute | solution.py:50
  430.2 25.2 %collective-permute-start.10 = (bf16[4,128,512]{2,1,0:T(8,128)(2,1)}, bf16[4,128,512]{2,1,0:T(8,128)(2,1)}, u32[]{:S(2)}, u32[]{:S(2)}) collective-permute-start(bf16[4,128,512]{2,1,0:T(8,128)(2,1)} %get-tuple-element.30), channel_id=1, source_target_pairs={{0,8},{1,9},{2,10},{3,11},{4,12},{5,13},{6,14},{7,15},{8,0},{9,1},... | collective-permute-start | bytes 1572872 | tf_op jit(solution)/shard_map/ppermute | solution.py:50
  433.5 25.6 %collective-permute-start.11 = (bf16[4,128,512]{2,1,0:T(8,128)(2,1)}, bf16[4,128,512]{2,1,0:T(8,128)(2,1)}, u32[]{:S(2)}, u32[]{:S(2)}) collective-permute-start(bf16[4,128,512]{2,1,0:T(8,128)(2,1)} %get-tuple-element.30), channel_id=1, source_target_pairs={{0,12},{1,13},{2,14},{3,15},{4,0},{5,1},{6,2},{7,3},{8,4},{9,5},{1... | collective-permute-start | bytes 1572872 | tf_op jit(solution)/shard_map/ppermute | solution.py:50
  462.4 15.9 %collective-permute-start.12 = (bf16[4,128,256]{2,1,0:T(8,128)(2,1)}, bf16[4,128,256]{2,1,0:T(8,128)(2,1)}, u32[]{:S(2)}, u32[]{:S(2)}) collective-permute-start(bf16[4,128,256]{2,1,0:T(8,128)(2,1)} %bitcast.34), channel_id=1, source_target_pairs={{0,12},{1,13},{2,14},{3,15},{4,0},{5,1},{6,2},{7,3},{8,4},{9,5},{1... | collective-permute-start | bytes 786440 | tf_op jit(solution)/shard_map/ppermute | solution.py:94
  465.8 16.0 %collective-permute-start.13 = (bf16[4,128,256]{2,1,0:T(8,128)(2,1)}, bf16[4,128,256]{2,1,0:T(8,128)(2,1)}, u32[]{:S(2)}, u32[]{:S(2)}) collective-permute-start(bf16[4,128,256]{2,1,0:T(8,128)(2,1)} %bitcast.36), channel_id=1, source_target_pairs={{0,8},{1,9},{2,10},{3,11},{4,12},{5,13},{6,14},{7,15},{8,0},{9,1},... | collective-permute-start | bytes 786440 | tf_op jit(solution)/shard_map/ppermute | solution.py:94
  468.6 14.6 %collective-permute-start.14 = (bf16[4,128,256]{2,1,0:T(8,128)(2,1)}, bf16[4,128,256]{2,1,0:T(8,128)(2,1)}, u32[]{:S(2)}, u32[]{:S(2)}) collective-permute-start(bf16[4,128,256]{2,1,0:T(8,128)(2,1)} %bitcast.38), channel_id=1, source_target_pairs={{0,4},{1,5},{2,6},{3,7},{4,8},{5,9},{6,10},{7,11},{8,12},{9,13},{1... | collective-permute-start | bytes 786440 | tf_op jit(solution)/shard_map/ppermute | solution.py:94
  471.8 25.9 %collective-permute-start.28 = (bf16[8,128,256]{2,1,0:T(8,128)(2,1)S(1)}, bf16[8,128,256]{2,1,0:T(8,128)(2,1)}, u32[]{:S(2)}, u32[]{:S(2)}) collective-permute-start(bf16[8,128,256]{2,1,0:T(8,128)(2,1)S(1)} %get-tuple-element.31), channel_id=1, source_target_pairs={{0,4},{1,5},{2,6},{3,7},{4,8},{5,9},{6,10},{7,11},{8,12},{9,13},{1... | collective-permute-start | bytes 1572872 | tf_op jit(solution)/shard_map/ppermute | solution.py:81
  476.4 29.1 %collective-permute-start.29 = (bf16[8,128,256]{2,1,0:T(8,128)(2,1)S(1)}, bf16[8,128,256]{2,1,0:T(8,128)(2,1)S(1)}, u32[]{:S(2)}, u32[]{:S(2)}) collective-permute-start(bf16[8,128,256]{2,1,0:T(8,128)(2,1)S(1)} %get-tuple-element.32), channel_id=1, source_target_pairs={{0,8},{1,9},{2,10},{3,11},{4,12},{5,13},{6,14},{7,15},{8,0},{9,1},... | collective-permute-start | bytes 1572872 | tf_op jit(solution)/shard_map/ppermute | solution.py:81
  478.3 27.9 %collective-permute-start.30 = (bf16[8,128,256]{2,1,0:T(8,128)(2,1)S(1)}, bf16[8,128,256]{2,1,0:T(8,128)(2,1)S(1)}, u32[]{:S(2)}, u32[]{:S(2)}) collective-permute-start(bf16[8,128,256]{2,1,0:T(8,128)(2,1)S(1)} %get-tuple-element.33), channel_id=1, source_target_pairs={{0,12},{1,13},{2,14},{3,15},{4,0},{5,1},{6,2},{7,3},{8,4},{9,5},{1... | collective-permute-start | bytes 1572872 | tf_op jit(solution)/shard_map/ppermute | solution.py:81
  484.5 27.1 %collective-permute-start.15 = (bf16[4,128,256]{2,1,0:T(8,128)(2,1)S(1)}, bf16[4,128,256]{2,1,0:T(8,128)(2,1)S(1)}, u32[]{:S(2)}, u32[]{:S(2)}) collective-permute-start(bf16[4,128,256]{2,1,0:T(8,128)(2,1)S(1)} %get-tuple-element.16), channel_id=1, source_target_pairs={{0,3},{1,0},{2,1},{3,2},{4,7},{5,4},{6,5},{7,6},{8,11},{9,8},{10,9... | collective-permute-start | bytes 786440 | tf_op jit(solution)/shard_map/ppermute | solution.py:98
  488.9 30.9 %collective-permute-start.16 = (bf16[4,128,256]{2,1,0:T(8,128)(2,1)S(1)}, bf16[4,128,256]{2,1,0:T(8,128)(2,1)S(1)}, u32[]{:S(2)}, u32[]{:S(2)}) collective-permute-start(bf16[4,128,256]{2,1,0:T(8,128)(2,1)S(1)} %get-tuple-element.18), channel_id=1, source_target_pairs={{0,2},{1,3},{2,0},{3,1},{4,6},{5,7},{6,4},{7,5},{8,10},{9,11},{10,... | collective-permute-start | bytes 786440 | tf_op jit(solution)/shard_map/ppermute | solution.py:98
  497.7 24.5 %collective-permute-start.17 = (bf16[4,128,256]{2,1,0:T(8,128)(2,1)S(1)}, bf16[4,128,256]{2,1,0:T(8,128)(2,1)S(1)}, u32[]{:S(2)}, u32[]{:S(2)}) collective-permute-start(bf16[4,128,256]{2,1,0:T(8,128)(2,1)S(1)} %get-tuple-element.15), channel_id=1, source_target_pairs={{0,1},{1,2},{2,3},{3,0},{4,5},{5,6},{6,7},{7,4},{8,9},{9,10},{10,1... | collective-permute-start | bytes 786440 | tf_op jit(solution)/shard_map/ppermute | solution.py:98
  527.2 3.3 copy-start.2
  530.5 2.7 copy-start.5
  531.2 35.9 %collective-permute-start.24 = (bf16[128,4096]{1,0:T(8,128)(2,1)S(1)}, bf16[128,4096]{1,0:T(8,128)(2,1)S(1)}, u32[]{:S(2)}, u32[]{:S(2)}) collective-permute-start(bf16[128,4096]{1,0:T(8,128)(2,1)S(1)} %add_convert_fusion), channel_id=1, source_target_pairs={{0,16},{16,32},{32,48},{48,64},{64,80},{80,96},{96,112},{112,128},... | collective-permute-start | bytes 3145736 | tf_op jit(solution)/shard_map/ppermute | solution.py:24
  533.2 33.1 %copy-start.7 = (bf16[1,256,768]{2,1,0:T(8,128)(2,1)S(1)}, bf16[1,256,768]{2,1,0:T(8,128)(2,1)}, u32[]{:S(2)}) copy-start(bf16[1,256,768]{2,1,0:T(8,128)(2,1)} %param.14) | copy-start | bytes 1179652
  535.6 30.7 %collective-permute-start.31 = (bf16[256,768]{1,0:T(8,128)(2,1)S(1)}, bf16[256,768]{1,0:T(8,128)(2,1)S(1)}, u32[]{:S(2)}, u32[]{:S(2)}) collective-permute-start(bf16[256,768]{1,0:T(8,128)(2,1)S(1)} %fusion.33), channel_id=1, source_target_pairs={{0,496},{16,480},{32,464},{48,448},{64,432},{80,416},{96,400},{112... | collective-permute-start | bytes 1179656 | tf_op jit(solution)/shard_map/ppermute | solution.py:29
  (8 other events, 17.4 us)
Sparse Core Ops, SparseCore 0:
  51.0 228.3 all-gather.1
